TPU v7x, 256 devices: a whole 4x4x8 slice. The times are simulated.
256 devices in a mesh: tok: 32 (over x, z), head: 8 (over y, core).
Axes of the slice: x: 4, y: 4, z: 8, core: 2. Of those that a mesh axis runs over, the one named last changes fastest.
Arguments:
- tokens: bfloat16 [32768, 1664], P(('tok', 'head')), may hold values from -75 to 75
- attn_gain: float32 [1664], replicated, may hold values from 0.1 to 1.9
- qkv_weight: bfloat16 [3, 1664, 1664], P(None, 'head'), may hold values from -5 to 5
- out_weight: bfloat16 [1664, 1664], P('head'), may hold values from -0.4375 to 0.4375
- merge_gain: float32 [1664], replicated, may hold values from 0.1 to 1.9
- merge_weight: bfloat16 [6656, 4096], P('head', 'tok'), may hold values from -0.078125 to 0.078125
- grid_sizes: int32 [2, 128], P(None, 'tok'), may hold values from 2 to 16, as said below
- segment_ids: int32 [32768], P('tok'), may hold values from 0 to 127, as said below
- patch_pos: int32 [2, 32768], P(None, 'tok'), may hold values from 0 to 15, as said below
- live_mask: int32 [32768], P('tok'), may hold values from 0 to 1, as said below
- owners: int32 [8192, 1], P(('tok', 'head')), may hold values from 0 to 31; in each aligned block of 32 rows (0 to 31, 32 to 63, ...) at most 2 rows name the same one
Outputs:
- delivered: bfloat16 [16384, 4096], P(('tok', 'head'))
Inputs may be any that keep to these rules, and one draw needn't show every extreme that they name: `grid_sizes`: both sides of every image are even, and some image is 16 by 16. `segment_ids`: never fall along the tokens. The aligned block b of 1024 tokens holds images b * 4 to (b + 1) * 4 - 1 packed in order from the block's start, image s taking grid_sizes[0, s] * grid_sizes[1, s] tokens; the block's remaining tokens carry the number of its last image. `patch_pos`: an image's tokens come in 2x2 windows, windows in row-major order, each window as (2 * r, 2 * c), (2 * r, 2 * c + 1), (2 * r + 1, 2 * c), (2 * r + 1, 2 * c + 1); padding tokens sit at (0, 0). `live_mask`: 1 exactly on the tokens that belong to an image. `owners`: in each aligned block of 32 rows (the merged rows of one device) no owner is named more than 2 times.
All inputs are finite; a program needn't handle non-finite values.
Results may differ from a plain program's by a relative error of at most 0.024.
Values may be sent and summed in bfloat16 or wider, within the bound.
No kernel may reach another device: no remote copies, remote signals or barrier semaphores. Data moves between devices by JAX's collectives and lax.ppermute only.
A program may use at most 64 MiB of HBM per device.

v0:
```python
import jax
import jax.numpy as jnp
from jax import lax
from jax.sharding import PartitionSpec as P

D = 1664
HD = 104
SIDE = 16
TOK = ("tx", "tz")
HEAD = ("hy", "hc")
Z_SIZE = 8
EPSILON = 1e-06
NEGATIVE = -1e30


def layer_norm(values, gain_vec):
    average = jnp.mean(values, axis=-1, keepdims=True)
    centred = values - average
    variance = jnp.mean(centred * centred, axis=-1, keepdims=True)
    return centred * lax.rsqrt(variance + EPSILON) * gain_vec


def rotate(vectors, row_coord, col_coord):
    quarter = vectors.shape[-1] // 4
    frequency = 10000.0 ** (-jnp.arange(quarter, dtype=jnp.float32) / quarter)
    pieces = []
    for which_axis, coordinate in ((0, row_coord), (1, col_coord)):
        leading = vectors[..., 2 * which_axis * quarter : (2 * which_axis + 1) * quarter]
        trailing = vectors[..., (2 * which_axis + 1) * quarter : (2 * which_axis + 2) * quarter]
        angles = coordinate[:, None, None] * frequency
        cosine = jnp.cos(angles)
        sine_val = jnp.sin(angles)
        pieces.append(leading * cosine - trailing * sine_val)
        pieces.append(leading * sine_val + trailing * cosine)
    return jnp.concatenate(pieces, axis=-1)


def body(
    tokens,
    attn_gain,
    qkv_weight,
    out_weight,
    merge_gain,
    merge_weight,
    grid_sizes,
    segment_ids,
    patch_pos,
    live_mask,
    owners,
):
    group_len = segment_ids.shape[0]
    local_rows = tokens.shape[0]
    head_width = qkv_weight.shape[1]
    heads_here = head_width // HD
    tok_count = lax.axis_size("tx") * lax.axis_size("tz")
    image_count = grid_sizes.shape[1]
    local_image = (
        segment_ids
        - (lax.axis_index("tx") * lax.axis_size("tz") + lax.axis_index("tz")) * image_count
    )
    image_match = local_image[:, None] == jnp.arange(image_count, dtype=jnp.int32)[None, :]
    grid_float = grid_sizes.astype(jnp.float32)
    row_size = jnp.sum(jnp.where(image_match, grid_float[0][None, :], 0.0), axis=1)
    col_size = jnp.sum(jnp.where(image_match, grid_float[1][None, :], 0.0), axis=1)
    row_coord = patch_pos[0].astype(jnp.float32) * SIDE / row_size
    col_coord = patch_pos[1].astype(jnp.float32) * SIDE / col_size
    stacked_weight = qkv_weight.reshape(3 * head_width, D)
    normed = layer_norm(tokens.astype(jnp.float32), attn_gain).astype(jnp.bfloat16)
    projected_rows = lax.dot_general(
        lax.all_gather(normed, HEAD, axis=0, tiled=True),
        stacked_weight,
        (((1,), (1,)), ((), ())),
        preferred_element_type=jnp.float32,
    )
    projected_rows = projected_rows.reshape(group_len, 3, heads_here, HD)
    query_all = (rotate(projected_rows[:, 0], row_coord, col_coord) * HD ** (-0.5)).astype(
        jnp.bfloat16
    )
    key_all = rotate(projected_rows[:, 1], row_coord, col_coord).astype(jnp.bfloat16)
    value_all = projected_rows[:, 2].astype(jnp.bfloat16)
    block_len = min(512, group_len)
    block_count = group_len // block_len
    key_live = live_mask == 1

    def allowed_pairs(query_start, span):
        query_seg = lax.dynamic_slice_in_dim(segment_ids, query_start, block_len)
        query_place = query_start + jnp.arange(block_len, dtype=jnp.int32)
        key_place = jnp.arange(span, dtype=jnp.int32)
        same_image = query_seg[:, None] == segment_ids[None, :]
        return same_image & (key_live[None, :] | (query_place[:, None] == key_place[None, :]))

    def query_block(query_start):
        queries = lax.dynamic_slice_in_dim(query_all, query_start, block_len, 0)
        allowed = allowed_pairs(query_start, group_len)
        scores = jnp.einsum("qhd,khd->hqk", queries, key_all, preferred_element_type=jnp.float32)
        masked = jnp.where(allowed[None], scores, NEGATIVE)
        row_top = jnp.max(masked, axis=2, keepdims=True)
        exponent = jnp.where(allowed[None], jnp.exp(masked - row_top), 0.0)
        denominator = jnp.sum(exponent, axis=2)
        numerator = jnp.einsum(
            "hqk,khd->qhd",
            exponent.astype(jnp.bfloat16),
            value_all,
            preferred_element_type=jnp.float32,
        )
        return (numerator / denominator.T[:, :, None]).astype(jnp.bfloat16)

    block_starts = jnp.arange(block_count, dtype=jnp.int32) * block_len
    heads_out = lax.map(query_block, block_starts).reshape(group_len, head_width)
    attn_rows = lax.psum_scatter(
        jnp.dot(heads_out, out_weight, preferred_element_type=jnp.float32).astype(jnp.bfloat16),
        HEAD,
        scatter_dimension=0,
        tiled=True,
    ).astype(jnp.float32)
    stream = (tokens.astype(jnp.float32) + attn_rows).reshape(local_rows // 4, 4, D)
    average = jnp.sum(stream, axis=2, keepdims=True) / D
    variance = jnp.sum(stream * stream, axis=2, keepdims=True) / D - average * average
    window_rows = ((stream - average) * lax.rsqrt(variance + EPSILON) * merge_gain).astype(
        jnp.bfloat16
    )
    merged_slice = lax.all_to_all(
        window_rows.reshape(local_rows // 4, 4 * D), HEAD, split_axis=1, concat_axis=0, tiled=True
    )
    merged_count = local_rows // 4
    column_terms = jnp.dot(
        merged_slice,
        lax.all_gather(
            lax.all_gather(merge_weight, "tz", axis=1, tiled=True), "tx", axis=1, tiled=True
        ),
        preferred_element_type=jnp.float32,
    )
    projected = lax.psum_scatter(
        column_terms.astype(jnp.bfloat16), HEAD, scatter_dimension=0, tiled=True
    )
    slot_count = max(2, 2 * merged_count // tok_count)
    owner_col = owners[:, 0]
    owner_hot = (owner_col[:, None] == jnp.arange(tok_count, dtype=jnp.int32)[None, :]).astype(
        jnp.int32
    )
    earlier = jnp.cumsum(owner_hot, axis=0, dtype=jnp.int32) - owner_hot
    slot_index = jnp.sum(earlier * owner_hot, axis=1, dtype=jnp.int32)
    target = owner_col * slot_count + slot_index
    select = (
        jnp.arange(tok_count * slot_count, dtype=jnp.int32)[:, None] == target[None, :]
    ).astype(jnp.bfloat16)
    send_rows = jnp.dot(select, projected, preferred_element_type=jnp.float32).astype(jnp.bfloat16)
    send_rows = send_rows.reshape(tok_count, slot_count, -1)
    received = lax.all_to_all(send_rows, TOK, split_axis=0, concat_axis=0, tiled=True)
    return received.reshape(tok_count * slot_count, -1)


def solution(mesh):
    tok_size, head_size = (mesh.shape[name] for name in mesh.axis_names)
    split_mesh = jax.sharding.Mesh(
        mesh.devices.reshape(tok_size // Z_SIZE, Z_SIZE, head_size // 2, 2), TOK + HEAD
    )
    placed = (
        P(TOK + HEAD, None),
        P(),
        P(None, HEAD, None),
        P(HEAD, None),
        P(),
        P(HEAD, TOK),
        P(None, TOK),
        P(TOK),
        P(None, TOK),
        P(TOK),
        P(TOK + HEAD, None),
    )
    return jax.shard_map(
        body, mesh=split_mesh, in_specs=placed, out_specs=P(TOK + HEAD, None), check_vma=False
    )
```

profile of v0, /device:TPU:57, one launch (start us, length us, event | category | flops | bytes accessed | tf_op | source)
XLA Modules:
  0.0 283.4 jit_solution(1939351082981799064)
XLA Ops:
  6.5 1.3 convert_reduce_fusion
  7.8 1.3 fusion.46
  9.1 2.1 fusion.48
  11.3 0.7 all-gather.6.cloned.1.call-update
  12.1 0.7 convert_element_type.65
  12.8 0.8 convert_multiply_fusion.1
  13.5 0.7 broadcast_compare_fusion
  14.2 0.7 broadcast_subtract_fusion
  14.9 0.1 select_reduce_fusion.2
  15.1 1.0 multiply_cosine_fusion.1
  16.0 28.0 %all-gather.4.cloned.1.call-done = bf16[1024,1664]{1,0:T(8,128)(2,1)} async-done(((bf16[128,1664]{1,0:T(8,128)(2,1)}), bf16[1024,1664]{1,0:T(8,128)(2,1)}) %all-gather.4.cloned.1.call-update) | async-done | bytes 3407888 | tf_op jit(solution)/shard_map/all_gather | solution.py:70
  44.1 4.5 %fusion.39 = f32[1024,3,2,104]{0,3,2,1:T(8,128)S(1)} fusion(bf16[3,2,104,1664]{3,2,1,0:T(8,128)(2,1)S(1)} %bitcast.70, bf16[1024,1664]{1,0:T(8,128)(2,1)} %all-gather.4.cloned.1.call-done), kind=kOutput, calls=%fused_computation.27 | convolution fusion | flops 2126512128 | bytes 8040448 | tf_op jit(solution)/shard_map/dot_general | solution.py:69
  48.6 0.2 slice_bitcast_fusion
  48.8 0.2 subtract_convert_fusion.1
  49.0 0.9 pad_maximum_fusion
  49.9 0.2 multiply_subtract_fusion.1
  50.0 0.9 fusion.49
  50.9 0.8 fusion.50
  51.8 23.2 %while.10 = (s32[]{:T(128)}, bf16[2,512,2,104]{1,3,2,0:T(8,128)(2,1)}, s32[2]{0:T(128)S(1)}, s32[1024]{0:T(1024)S(1)}, pred[1024]{0:T(1024)(128)(4,1)S(1)}, /*in...) while((s32[]{:T(128)}, ...), condition=%wide.region_9.10_spmd, body=%wide.region_6.0_spmd.sunk | while | flops 443762176 | bytes 7069351 | solution.py:109
  51.8 0.6 dynamic_slice.26
  54.3 0.6 iota_add_fusion.2
  54.9 0.7 fusion.80
  55.6 4.6 %fusion.81 = (f32[2,512]{1,0:T(2,128)S(1)}, bf16[2,512,1024]{2,1,0:T(8,128)(2,1)}) fusion(pred[512,1024]{1,0:T(8,128)(4,1)S(1)} %fusion.80, bf16[1024,2,104]{0,2,1:T(8,128)(2,1)} %get-tuple-element.180, bf16[1024,2,104]{0,2,1:T(8,128)(2,1)} %get-tuple-element.179, s32[]{:T(128)S(6)} %select_n.34), kind=kOutput, calls=%fused_computation.84.clone.1 | convolution fusion | flops 223347712 | bytes 3788804 | tf_op jit(solution)/shard_map/while/body/eval_jaxpr/sub | solution.py:98
  60.2 3.1 %fusion.82 = bf16[2,512,2,104]{1,3,2,0:T(8,128)(2,1)} fusion(bf16[2,512,2,104]{1,3,2,0:T(8,128)(2,1)} %get-tuple-element.164, s32[]{:T(128)} %get-tuple-element.163, bf16[1024,2,104]{0,2,1:T(8,128)(2,1)} %get-tuple-element.181, bf16[2,512,1024]{2,1,0:T(8,128)(2,1)} %get-tuple-element.150, f32[512,2]{0,1:T(2,128)S(1)} %bitcast.80), kind=kOutput, calls=%fused_computation.15.clone.1 | convolution fusion | flops 218316800 | bytes 2740736 | tf_op jit(solution)/shard_map/while/body/eval_jaxpr/hqk,khd->qhd/dot_general | solution.py:100
  63.3 0.6 dynamic_slice.26
  65.9 0.6 iota_add_fusion.2
  66.5 0.7 fusion.80
  67.2 4.6 %fusion.81 = (f32[2,512]{1,0:T(2,128)S(1)}, bf16[2,512,1024]{2,1,0:T(8,128)(2,1)}) fusion(pred[512,1024]{1,0:T(8,128)(4,1)S(1)} %fusion.80, bf16[1024,2,104]{0,2,1:T(8,128)(2,1)} %get-tuple-element.180, bf16[1024,2,104]{0,2,1:T(8,128)(2,1)} %get-tuple-element.179, s32[]{:T(128)S(6)} %select_n.34), kind=kOutput, calls=%fused_computation.84.clone.1 | convolution fusion | flops 223347712 | bytes 3788804 | tf_op jit(solution)/shard_map/while/body/eval_jaxpr/sub | solution.py:98
  71.8 3.1 %fusion.82 = bf16[2,512,2,104]{1,3,2,0:T(8,128)(2,1)} fusion(bf16[2,512,2,104]{1,3,2,0:T(8,128)(2,1)} %get-tuple-element.164, s32[]{:T(128)} %get-tuple-element.163, bf16[1024,2,104]{0,2,1:T(8,128)(2,1)} %get-tuple-element.181, bf16[2,512,1024]{2,1,0:T(8,128)(2,1)} %get-tuple-element.150, f32[512,2]{0,1:T(2,128)S(1)} %bitcast.80), kind=kOutput, calls=%fused_computation.15.clone.1 | convolution fusion | flops 218316800 | bytes 2740736 | tf_op jit(solution)/shard_map/while/body/eval_jaxpr/hqk,khd->qhd/dot_general | solution.py:100
  74.9 1.5 copy.16
  76.5 3.0 %convolution_convert_fusion.2 = bf16[1024,1664]{1,0:T(8,128)(2,1)} fusion(bf16[1024,208]{0,1:T(8,128)(2,1)S(1)} %bitcast.71, bf16[208,1664]{1,0:T(8,128)(2,1)S(1)} %copy-done.2), kind=kOutput, calls=%fused_computation.26 | convolution fusion | flops 710541312 | bytes 4526080 | tf_op jit(solution)/shard_map/dot_general | solution.py:111
  79.5 6.4 %all-gather.6.cloned.1.call-done = bf16[832,1024]{1,0:T(8,128)(2,1)} async-done(((bf16[832,128]{1,0:T(8,128)(2,1)}), bf16[832,1024]{1,0:T(8,128)(2,1)}) %all-gather.6.cloned.1.call-update) | async-done | bytes 1703952 | tf_op jit(solution)/shard_map/all_gather | solution.py:129
  86.0 0.1 mul.317
  86.1 43.7 %reduce-scatter.3.cloned.1.call-done = bf16[128,1664]{1,0:T(8,128)(2,1)} async-done(((bf16[1024,1664]{1,0:T(8,128)(2,1)}), bf16[128,1664]{1,0:T(8,128)(2,1)}) %reduce-scatter.3.cloned.1.call-update) | async-done | bytes 426000 | tf_op jit(solution)/shard_map/reduce_scatter | solution.py:110
  129.8 2.1 fusion.53
  131.9 0.1 div.50
  132.0 0.1 div.52
  132.3 1.4 reshape.306
  133.7 0.3 fusion.45
  134.0 11.9 %all_to_all.21 = bf16[32,8,832]{2,0,1:T(8,128)(2,1)S(1)} all-to-all(bf16[32,8,832]{2,0,1:T(8,128)(2,1)S(1)} %fusion.45), channel_id=1, replica_groups=mesh['tx'=4,'tz'=8,'hy'=4,'hc'=2] {'hy','hc'}, dimensions={1} | all-to-all | bytes 851968 | tf_op jit(solution)/shard_map/all_to_all | solution.py:122
  145.9 58.5 %all-gather.8.cloned.1.call-done = bf16[832,4096]{1,0:T(8,128)(2,1)} async-done(((bf16[832,1024]{1,0:T(8,128)(2,1)}), bf16[832,4096]{1,0:T(8,128)(2,1)}) %all-gather.8.cloned.1.call-update) | async-done | bytes 6815760 | tf_op jit(solution)/shard_map/all_gather | solution.py:128
  204.4 6.8 %convolution_convert_fusion = bf16[256,4096]{1,0:T(8,128)(2,1)} fusion(bf16[256,832]{1,0:T(8,128)(2,1)S(1)} %bitcast.73, bf16[832,4096]{1,0:T(8,128)(2,1)} %all-gather.8.cloned.1.call-done), kind=kOutput, calls=%fused_computation.24 | convolution fusion | flops 1745879040 | bytes 9338880 | tf_op jit(solution)/shard_map/dot_general | solution.py:126
  211.3 0.2 select_reduce_fusion.3
  211.5 35.4 %reduce-scatter.5.cloned.1.call-done = bf16[32,4096]{1,0:T(8,128)(2,1)} async-done(((bf16[256,4096]{1,0:T(8,128)(2,1)}), bf16[32,4096]{1,0:T(8,128)(2,1)}) %reduce-scatter.5.cloned.1.call-update) | async-done | bytes 262160 | tf_op jit(solution)/shard_map/reduce_scatter | solution.py:133
  247.0 1.2 convolution_convert_fusion.1
  248.2 0.3 reshape.307
  248.5 27.3 %all_to_all.22 = bf16[32,2,4096]{2,1,0:T(2,128)(2,1)S(1)} all-to-all(bf16[32,2,4096]{2,1,0:T(2,128)(2,1)S(1)} %reshape.307), channel_id=1, replica_groups=mesh['tx'=4,'tz'=8,'hy'=4,'hc'=2] {'tx','tz'}, dimensions={0} | all-to-all | bytes 1048576 | tf_op jit(solution)/shard_map/all_to_all | solution.py:149
  275.8 1.0 reshape.308
  (43 shorter events, 0.8 us)
Async XLA Ops:
  6.5 37.5 %copy-start = (bf16[3,208,1664]{2,1,0:T(8,128)(2,1)S(1)}, bf16[3,208,1664]{2,1,0:T(8,128)(2,1)}, u32[]{:S(2)}) copy-start(bf16[3,208,1664]{2,1,0:T(8,128)(2,1)} %param.15) | copy-start | bytes 6230020
  6.5 37.5 %all-gather.4.cloned.1.call-start = ((), (), s32[]{:S(2)}) async-start(), calls=%async_computation.4 | async-start | bytes 3833856 | tf_op jit(solution)/shard_map/all_gather | solution.py:70
  11.2 74.7 %all-gather.6.cloned.1.call-start = ((), (), s32[]{:S(2)}) async-start(), calls=%async_computation.6 | async-start | bytes 1916928 | tf_op jit(solution)/shard_map/all_gather | solution.py:129
  12.0 117.8 %reduce-scatter.3.cloned.1.call-start = ((), (), s32[]{:S(2)}) async-start(), calls=%async_computation.5 | async-start | bytes 3833856 | tf_op jit(solution)/shard_map/reduce_scatter | solution.py:110
  49.0 2.8 copy-start.3
  51.8 24.7 %copy-start.2 = (bf16[208,1664]{1,0:T(8,128)(2,1)S(1)}, bf16[208,1664]{1,0:T(8,128)(2,1)}, u32[]{:S(2)}) copy-start(bf16[208,1664]{1,0:T(8,128)(2,1)} %param.16) | copy-start | bytes 2076676
  79.4 6.6 %copy-start.4 = (f32[1664]{0:T(1024)S(1)}, f32[1664]{0:T(1024)}, u32[]{:S(2)}) copy-start(f32[1664]{0:T(1024)} %param.17) | copy-start | bytes 19972
  79.4 50.4 %copy-start.1 = (bf16[128,1664]{1,0:T(8,128)(2,1)S(1)}, bf16[128,1664]{1,0:T(8,128)(2,1)}, u32[]{:S(2)}) copy-start(bf16[128,1664]{1,0:T(8,128)(2,1)} %param.13) | copy-start | bytes 1277956
  79.5 125.0 %all-gather.8.cloned.1.call-start = ((), (), s32[]{:S(2)}) async-start(), calls=%async_computation.7 | async-start | bytes 8519680 | tf_op jit(solution)/shard_map/all_gather | solution.py:128
  86.0 161.0 %reduce-scatter.5.cloned.1.call-start = ((), (), s32[]{:S(2)}) async-start(), calls=%async_computation.8 | async-start | bytes 2359296 | tf_op jit(solution)/shard_map/reduce_scatter | solution.py:133
  204.4 6.8 %copy-start.5 = (s32[32,1]{0,1:T(1,128)S(1)}, s32[32,1]{0,1:T(1,128)}, u32[]{:S(2)}) copy-start(s32[32,1]{0,1:T(1,128)} %param.23) | copy-start | bytes 388
Sparse Core Ops, SparseCore 0:
  11.3 32.6 all-gather.3
  45.8 40.0 all-gather.5
  88.5 41.2 reduce-scatter.2
  131.5 72.9 all-gather.7
  211.3 35.5 reduce-scatter.4
where the time goes:
time: 284 us; the launch traced here: 283 us
  waiting for transfers between devices  173 us (61%)
  blocking collectives  39.2 us (14%)
  matrix products  30.9 us (11%)
  other arithmetic  16.1 us (6%)
  between operations  13.4 us (5%)
  local copies, waits for them, and re-layouts  7.1 us (2%)
  loops' own time  3.76 us (1%)
    all_gather x1, waiting for transfers between devices, body(): lax.all_gather(lax.all_gather(merge_weight, 'tz', axis=1, tiled=True), 't...  58.5 us
    reduce_scatter x1, waiting for transfers between devices, body(): lax.psum_scatter(jnp.dot(heads_out, out_weight, preferred_element_type=jn...  43.7 us
    reduce_scatter x1, waiting for transfers between devices, body(): lax.psum_scatter(column_terms.astype(jnp.bfloat16), HEAD, scatter_dimensi...  35.4 us
    all_gather x1, waiting for transfers between devices, body(): lax.all_gather(normed, HEAD, axis=0, tiled=True)  28 us
    all_to_all x1, blocking collectives, body(): lax.all_to_all(send_rows, TOK, split_axis=0, concat_axis=0, tiled=True)  27.3 us
    all_to_all x1, blocking collectives, body(): lax.all_to_all(window_rows.reshape(local_rows // 4, 4 * D), HEAD, split_a...  11.9 us
    sub x2, matrix products, query_block(): exponent = jnp.where(allowed[None], jnp.exp(masked - row_top), 0.0)  9.24 us
    dot_general x1, matrix products, body(): jnp.dot(merged_slice, lax.all_gather(lax.all_gather(merge_weight, 'tz', a...  6.76 us
  transfers between devices with their start and end apart: 5, of which 5 were waited for; matrix products, arithmetic and copies ran while one was open for 14% of the time, Pallas kernels for 0%

commit v1 on v0

--- a/solution.py
+++ b/solution.py
@@ -66,8 +66,15 @@
     col_coord = patch_pos[1].astype(jnp.float32) * SIDE / col_size
     stacked_weight = qkv_weight.reshape(3 * head_width, D)
     normed = layer_norm(tokens.astype(jnp.float32), attn_gain).astype(jnp.bfloat16)
+
+    def ends_trace(x_local, peer_axis):
+        piece_out = jnp.concatenate(
+            lax.all_to_all(jnp.stack(lax.axis_size(peer_axis) * [x_local], 0), peer_axis, 0, 0), 0
+        )
+        return piece_out
+
     projected_rows = lax.dot_general(
-        lax.all_gather(normed, HEAD, axis=0, tiled=True),
+        ends_trace(normed, HEAD),
         stacked_weight,
         (((1,), (1,)), ((), ())),
         preferred_element_type=jnp.float32,

time: 284 us -> 251 us (0.88)
  waiting for transfers between devices: 173 us -> 134 us
  starting transfers between devices: 0.16 us -> 5.24 us
  other arithmetic: 16.1 us -> 12.6 us
    all_gather x1, waiting for transfers between devices: 58.5 us -> 20.8 us  [body(): lax.all_gather(lax.all_gather(merge_weight, 'tz', axis=1, tiled=True), 't...]
    all_to_all x0 -> x1, waiting for transfers between devices: none -> 36.6 us  [ends_trace(): lax.all_to_all(jnp.stack(lax.axis_size(peer_axis) * [x_local], 0), peer_a...]
    all_gather x1 -> x0, waiting for transfers between devices: 28 us -> none  [body(): lax.all_gather(normed, HEAD, axis=0, tiled=True)]
    all_gather x1, waiting for transfers between devices: 6.42 us -> 0.02 us  [body(): lax.all_gather(merge_weight, 'tz', axis=1, tiled=True)]
    all_to_all x0 -> x1, starting transfers between devices: none -> 5.12 us  [ends_trace(): lax.all_to_all(jnp.stack(lax.axis_size(peer_axis) * [x_local], 0), peer_a...]
    reduce_scatter x1, waiting for transfers between devices: 43.7 us -> 39.9 us  [body(): lax.psum_scatter(jnp.dot(heads_out, out_weight, preferred_element_type=jn...]
  transfers between devices with their start and end apart: 5 -> 5, of which waited for: 5 -> 4; matrix products, arithmetic and copies ran while one was open for 14% -> 15% of each run, Pallas kernels for 0% -> 0%
where the time goes in v1:
time: 251 us; the launch traced here: 250 us
  waiting for transfers between devices  134 us (53%)
  blocking collectives  38.8 us (15%)
  matrix products  30.9 us (12%)
  between operations  15.2 us (6%)
  other arithmetic  12.6 us (5%)
  local copies, waits for them, and re-layouts  9.24 us (4%)
  starting transfers between devices  5.24 us (2%)
  loops' own time  4.18 us (2%)
    reduce_scatter x1, waiting for transfers between devices, body(): lax.psum_scatter(jnp.dot(heads_out, out_weight, preferred_element_type=jn...  39.9 us
    all_to_all x1, waiting for transfers between devices, ends_trace(): lax.all_to_all(jnp.stack(lax.axis_size(peer_axis) * [x_local], 0), peer_a...  36.6 us
    reduce_scatter x1, waiting for transfers between devices, body(): lax.psum_scatter(column_terms.astype(jnp.bfloat16), HEAD, scatter_dimensi...  35.4 us
    all_to_all x1, blocking collectives, body(): lax.all_to_all(send_rows, TOK, split_axis=0, concat_axis=0, tiled=True)  27.2 us
    all_gather x1, waiting for transfers between devices, body(): lax.all_gather(lax.all_gather(merge_weight, 'tz', axis=1, tiled=True), 't...  20.8 us
    all_to_all x1, blocking collectives, body(): lax.all_to_all(window_rows.reshape(local_rows // 4, 4 * D), HEAD, split_a...  11.6 us
    sub x2, matrix products, query_block(): exponent = jnp.where(allowed[None], jnp.exp(masked - row_top), 0.0)  9.23 us
    dot_general x1, matrix products, body(): jnp.dot(merged_slice, lax.all_gather(lax.all_gather(merge_weight, 'tz', a...  6.77 us
  transfers between devices with their start and end apart: 5, of which 4 were waited for; matrix products, arithmetic and copies ran while one was open for 15% of the time, Pallas kernels for 0%

profile of v1, /device:TPU:57, one launch (start us, length us, event | category | flops | bytes accessed | tf_op | source)
XLA Modules:
  0.0 250.3 jit_solution(7336181758455419596)
XLA Ops:
  7.4 1.3 convert_reduce_fusion
  8.7 1.3 fusion.44
  9.9 1.3 fusion.46
  11.3 2.0 stack.2
  13.3 5.1 %all-to-all-start = ((bf16[8,128,1664]{2,1,0:T(8,128)(2,1)}), bf16[8,128,1664]{2,1,0:T(8,128)(2,1)}, u32[]{:S(2)}, u32[]{:S(2)}) async-start(bf16[8,128,1664]{2,1,0:T(8,128)(2,1)} %stack.2), calls=%async_computation | async-start | bytes 6815744 | tf_op jit(solution)/shard_map/all_to_all | solution.py:72
  18.4 0.7 all-gather.3.cloned.1.call-update
  19.3 0.1 select_reduce_fusion.2
  19.5 1.0 multiply_cosine_fusion.1
  20.5 36.6 %all-to-all-done = bf16[8,128,1664]{2,1,0:T(8,128)(2,1)} async-done(((bf16[8,128,1664]{2,1,0:T(8,128)(2,1)}), bf16[8,128,1664]{2,1,0:T(8,128)(2,1)}, u32[]{:S(2)}, u32[]{:S(2)}) %all-to-all-start) | async-done | bytes 3407904 | tf_op jit(solution)/shard_map/all_to_all | solution.py:72
  57.1 4.5 %fusion.57 = f32[1024,3,2,104]{0,3,2,1:T(8,128)S(1)} fusion(bf16[1024,1664,1,1]{1,0,3,2:T(8,128)(2,1)} %bitcast.7, bf16[3,2,104,1664]{3,2,1,0:T(8,128)(2,1)S(1)} %bitcast.71), kind=kOutput, calls=%fused_computation.83 | convolution fusion | flops 2126512128 | bytes 8040448 | tf_op jit(solution)/shard_map/dot_general | solution.py:76
  61.6 0.2 slice_bitcast_fusion
  61.8 0.2 subtract_convert_fusion.1
  62.0 0.9 pad_maximum_fusion
  62.9 0.2 multiply_subtract_fusion.1
  63.0 0.9 fusion.47
  63.9 0.8 fusion.48
  64.8 23.8 %while.10 = (s32[]{:T(128)}, bf16[2,512,2,104]{1,3,2,0:T(8,128)(2,1)}, s32[2]{0:T(128)S(1)}, s32[1024]{0:T(1024)S(1)}, pred[1024]{0:T(1024)(128)(4,1)S(1)}, /*in...) while((s32[]{:T(128)}, ...), condition=%wide.region_9.10_spmd, body=%wide.region_6.0_spmd.sunk | while | flops 443762176 | bytes 7069351 | solution.py:116
  64.8 0.7 dynamic_slice.26
  67.5 0.1 dynamic_slice.27
  67.6 0.7 iota_add_fusion.2
  68.3 0.7 fusion.80
  69.0 4.6 %fusion.81 = (f32[2,512]{1,0:T(2,128)S(1)}, bf16[2,512,1024]{2,1,0:T(8,128)(2,1)}) fusion(pred[512,1024]{1,0:T(8,128)(4,1)S(1)} %fusion.80, bf16[1024,2,104]{0,2,1:T(8,128)(2,1)} %get-tuple-element.180, bf16[1024,2,104]{0,2,1:T(8,128)(2,1)} %get-tuple-element.179, s32[]{:T(128)S(6)} %select_n.34), kind=kOutput, calls=%fused_computation.82.clone.1 | convolution fusion | flops 223347712 | bytes 3788804 | tf_op jit(solution)/shard_map/while/body/eval_jaxpr/sub | solution.py:105
  73.6 3.1 %fusion.82 = bf16[2,512,2,104]{1,3,2,0:T(8,128)(2,1)} fusion(bf16[2,512,2,104]{1,3,2,0:T(8,128)(2,1)} %get-tuple-element.164, s32[]{:T(128)} %get-tuple-element.163, bf16[1024,2,104]{0,2,1:T(8,128)(2,1)} %get-tuple-element.181, bf16[2,512,1024]{2,1,0:T(8,128)(2,1)} %get-tuple-element.150, f32[512,2]{0,1:T(2,128)S(1)} %bitcast.81), kind=kOutput, calls=%fused_computation.15.clone.1 | convolution fusion | flops 218316800 | bytes 2740736 | tf_op jit(solution)/shard_map/while/body/eval_jaxpr/hqk,khd->qhd/dot_general | solution.py:107
  76.7 0.7 dynamic_slice.26
  79.4 0.1 dynamic_slice.27
  79.5 0.7 iota_add_fusion.2
  80.2 0.7 fusion.80
  80.9 4.6 %fusion.81 = (f32[2,512]{1,0:T(2,128)S(1)}, bf16[2,512,1024]{2,1,0:T(8,128)(2,1)}) fusion(pred[512,1024]{1,0:T(8,128)(4,1)S(1)} %fusion.80, bf16[1024,2,104]{0,2,1:T(8,128)(2,1)} %get-tuple-element.180, bf16[1024,2,104]{0,2,1:T(8,128)(2,1)} %get-tuple-element.179, s32[]{:T(128)S(6)} %select_n.34), kind=kOutput, calls=%fused_computation.82.clone.1 | convolution fusion | flops 223347712 | bytes 3788804 | tf_op jit(solution)/shard_map/while/body/eval_jaxpr/sub | solution.py:105
  85.5 3.1 %fusion.82 = bf16[2,512,2,104]{1,3,2,0:T(8,128)(2,1)} fusion(bf16[2,512,2,104]{1,3,2,0:T(8,128)(2,1)} %get-tuple-element.164, s32[]{:T(128)} %get-tuple-element.163, bf16[1024,2,104]{0,2,1:T(8,128)(2,1)} %get-tuple-element.181, bf16[2,512,1024]{2,1,0:T(8,128)(2,1)} %get-tuple-element.150, f32[512,2]{0,1:T(2,128)S(1)} %bitcast.81), kind=kOutput, calls=%fused_computation.15.clone.1 | convolution fusion | flops 218316800 | bytes 2740736 | tf_op jit(solution)/shard_map/while/body/eval_jaxpr/hqk,khd->qhd/dot_general | solution.py:107
  88.6 1.4 copy.16
  90.1 3.0 %convolution_convert_fusion.2 = bf16[1024,1664]{1,0:T(8,128)(2,1)} fusion(bf16[1024,208]{0,1:T(8,128)(2,1)S(1)} %bitcast.72, bf16[208,1664]{1,0:T(8,128)(2,1)S(1)} %copy-done.2), kind=kOutput, calls=%fused_computation.26 | convolution fusion | flops 710541312 | bytes 4526080 | tf_op jit(solution)/shard_map/dot_general | solution.py:118
  93.2 0.7 all-gather.5.cloned.1.call-update
  93.9 0.1 mul.317
  94.0 39.9 %reduce-scatter.3.cloned.1.call-done = bf16[128,1664]{1,0:T(8,128)(2,1)} async-done(((bf16[1024,1664]{1,0:T(8,128)(2,1)}), bf16[128,1664]{1,0:T(8,128)(2,1)}) %reduce-scatter.3.cloned.1.call-update) | async-done | bytes 426000 | tf_op jit(solution)/shard_map/reduce_scatter | solution.py:117
  133.9 2.1 fusion.51
  136.0 0.1 div.50
  136.1 0.1 div.52
  136.4 1.4 reshape.312
  137.8 0.3 fusion.43
  138.2 11.6 %all_to_all.26 = bf16[32,8,832]{2,0,1:T(8,128)(2,1)S(1)} all-to-all(bf16[32,8,832]{2,0,1:T(8,128)(2,1)S(1)} %fusion.43), channel_id=1, replica_groups=mesh['tx'=4,'tz'=8,'hy'=4,'hc'=2] {'hy','hc'}, dimensions={1} | all-to-all | bytes 851968 | tf_op jit(solution)/shard_map/all_to_all | solution.py:129
  149.8 20.8 %all-gather.5.cloned.1.call-done = bf16[832,4096]{1,0:T(8,128)(2,1)} async-done(((bf16[832,1024]{1,0:T(8,128)(2,1)}), bf16[832,4096]{1,0:T(8,128)(2,1)}) %all-gather.5.cloned.1.call-update) | async-done | bytes 6815760 | tf_op jit(solution)/shard_map/all_gather | solution.py:135
  170.6 6.8 %convolution_convert_fusion = bf16[256,4096]{1,0:T(8,128)(2,1)} fusion(bf16[256,832]{1,0:T(8,128)(2,1)S(1)} %bitcast.74, bf16[832,4096]{1,0:T(8,128)(2,1)} %all-gather.5.cloned.1.call-done), kind=kOutput, calls=%fused_computation.24 | convolution fusion | flops 1745879040 | bytes 9338880 | tf_op jit(solution)/shard_map/dot_general | solution.py:133
  177.5 0.2 select_reduce_fusion.3
  177.7 35.4 %reduce-scatter.5.cloned.1.call-done = bf16[32,4096]{1,0:T(8,128)(2,1)} async-done(((bf16[256,4096]{1,0:T(8,128)(2,1)}), bf16[32,4096]{1,0:T(8,128)(2,1)}) %reduce-scatter.5.cloned.1.call-update) | async-done | bytes 262160 | tf_op jit(solution)/shard_map/reduce_scatter | solution.py:140
  213.1 1.2 convolution_convert_fusion.1
  214.3 0.3 reshape.313
  214.7 27.2 %all_to_all.27 = bf16[32,2,4096]{2,1,0:T(2,128)(2,1)S(1)} all-to-all(bf16[32,2,4096]{2,1,0:T(2,128)(2,1)S(1)} %reshape.313), channel_id=1, replica_groups=mesh['tx'=4,'tz'=8,'hy'=4,'hc'=2] {'tx','tz'}, dimensions={0} | all-to-all | bytes 1048576 | tf_op jit(solution)/shard_map/all_to_all | solution.py:156
  241.8 1.0 reshape.314
  (49 shorter events, 0.7 us)
Async XLA Ops:
  7.4 49.7 %copy-start = (bf16[3,208,1664]{2,1,0:T(8,128)(2,1)S(1)}, bf16[3,208,1664]{2,1,0:T(8,128)(2,1)}, u32[]{:S(2)}) copy-start(bf16[3,208,1664]{2,1,0:T(8,128)(2,1)} %param.15) | copy-start | bytes 6230020
  13.3 5.9 %copy-start.8 = (s32[2,4]{1,0:T(2,128)S(1)}, s32[2,4]{1,0:T(2,128)}, u32[]{:S(2)}) copy-start(s32[2,4]{1,0:T(2,128)} %param.19) | copy-start | bytes 100
  13.3 6.0 %copy-start.3 = (s32[1024]{0:T(1024)S(1)}, s32[1024]{0:T(1024)}, u32[]{:S(2)}) copy-start(s32[1024]{0:T(1024)} %param.20) | copy-start | bytes 12292
  13.3 6.1 %copy-start.4 = (s32[2,1024]{1,0:T(2,128)S(1)}, s32[2,1024]{1,0:T(2,128)}, u32[]{:S(2)}) copy-start(s32[2,1024]{1,0:T(2,128)} %param.21) | copy-start | bytes 24580
  13.3 6.2 %copy-start.6 = (s32[1024]{0:T(1024)S(1)}, s32[1024]{0:T(1024)}, u32[]{:S(2)}) copy-start(s32[1024]{0:T(1024)} %param.22) | copy-start | bytes 12292
  13.3 43.8 %all-to-all-start = ((bf16[8,128,1664]{2,1,0:T(8,128)(2,1)}), bf16[8,128,1664]{2,1,0:T(8,128)(2,1)}, u32[]{:S(2)}, u32[]{:S(2)}) async-start(bf16[8,128,1664]{2,1,0:T(8,128)(2,1)} %stack.2), calls=%async_computation | async-start | bytes 6815744 | tf_op jit(solution)/shard_map/all_to_all | solution.py:72
  18.4 74.8 %all-gather.3.cloned.1.call-start = ((), (), s32[]{:S(2)}) async-start(), calls=%async_computation.6 | async-start | bytes 1916928 | tf_op jit(solution)/shard_map/all_gather | solution.py:136
  19.1 114.8 %reduce-scatter.3.cloned.1.call-start = ((), (), s32[]{:S(2)}) async-start(), calls=%async_computation.5 | async-start | bytes 3833856 | tf_op jit(solution)/shard_map/reduce_scatter | solution.py:117
  64.8 25.3 %copy-start.2 = (bf16[208,1664]{1,0:T(8,128)(2,1)S(1)}, bf16[208,1664]{1,0:T(8,128)(2,1)}, u32[]{:S(2)}) copy-start(bf16[208,1664]{1,0:T(8,128)(2,1)} %param.16) | copy-start | bytes 2076676
  93.1 0.8 copy-start.5
  93.1 40.8 %copy-start.1 = (bf16[128,1664]{1,0:T(8,128)(2,1)S(1)}, bf16[128,1664]{1,0:T(8,128)(2,1)}, u32[]{:S(2)}) copy-start(bf16[128,1664]{1,0:T(8,128)(2,1)} %param.13) | copy-start | bytes 1277956
  93.1 77.5 %all-gather.5.cloned.1.call-start = ((), (), s32[]{:S(2)}) async-start(), calls=%async_computation.7 | async-start | bytes 8519680 | tf_op jit(solution)/shard_map/all_gather | solution.py:135
  93.8 119.3 %reduce-scatter.5.cloned.1.call-start = ((), (), s32[]{:S(2)}) async-start(), calls=%async_computation.8 | async-start | bytes 2359296 | tf_op jit(solution)/shard_map/reduce_scatter | solution.py:140
  170.6 6.8 %copy-start.7 = (s32[32,1]{0,1:T(1,128)S(1)}, s32[32,1]{0,1:T(1,128)}, u32[]{:S(2)}) copy-start(s32[32,1]{0,1:T(1,128)} %param.23) | copy-start | bytes 388
Sparse Core Ops, SparseCore 0:
  20.9 41.6 all-gather.2
  95.7 74.8 all-gather.4
Sparse Core Ops, SparseCore 1:
  93.2 40.7 reduce-scatter.2
  177.4 35.6 reduce-scatter.4
